TPU v7x, 32 devices: a whole 2x2x4 slice. The times are simulated.
32 devices in a mesh: sky: 8 (over z, y), los: 4 (over x, core).
Axes of the slice: x: 2, y: 2, z: 4, core: 2. Of those that a mesh axis runs over, the one named last changes fastest.
Arguments:
- features: bfloat16 [32, 16, 32, 128], P(None, 'sky', 'los'), may hold values from -6 to 6
- pre_first: bfloat16 [32, 16, 32, 128], P(None, 'sky', 'los'), may hold values from -8 to 8
- pre_second: bfloat16 [32, 16, 32, 128], P(None, 'sky', 'los'), may hold values from -8 to 8
- w_first: bfloat16 [3, 3, 3, 32, 32], replicated, may hold values from -0.21875 to 0.21875
- w_second: bfloat16 [3, 3, 3, 32, 32], replicated, may hold values from -0.21875 to 0.21875
- w_out: bfloat16 [3, 32], replicated, may hold values from -1 to 1
- b_out: float32 [3], replicated, may hold values from -1 to 1
- y_target: float32 [16, 128], P('sky'), may hold values from -6 to 6
- k_target: float32 [16, 128], P('sky'), may hold values from -6 to 6
Outputs:
- grad_features: bfloat16 [32, 16, 32, 128], P(None, 'sky', 'los')
- grad_first: float32 [3, 3, 3, 32, 32], replicated
- grad_second: float32 [3, 3, 3, 32, 32], replicated
- grad_out: float32 [3, 32], replicated
- grad_bias: float32 [3], replicated
All inputs are finite; a program needn't handle non-finite values.
Results may differ from a plain program's by a relative error of at most 0.0067.
Values may be sent and summed in bfloat16 or wider, within the bound.
No kernel may reach another device: no remote copies, remote signals or barrier semaphores. Data moves between devices by JAX's collectives and lax.ppermute only.
A program may use at most 64 MiB of HBM per device.

v0:
```python
import math
import jax
import jax.numpy as jnp
from jax import lax
from jax.sharding import PartitionSpec as P


def extended(block, sides, width):
    for axis, dim in sides:
        count = lax.axis_size(axis)
        forward = [(i, i + 1) for i in range(count - 1)]
        forward.append((count - 1, 0))
        backward = [(target, source) for source, target in forward]
        low = lax.ppermute(
            lax.slice_in_dim(block, block.shape[dim] - width, None, axis=dim), axis, forward
        )
        high = lax.ppermute(lax.slice_in_dim(block, 0, width, axis=dim), axis, backward)
        block = jnp.concatenate([low, block, high], axis=dim)
    return block


def silu_slope(value):
    sigma = jax.nn.sigmoid(value)
    return sigma * (1.0 + value * (1.0 - sigma))


def wrap_columns(field):
    return jnp.concatenate((field[..., -1:], field, field[..., :1]), axis=-1)


def spread_local(weight, padded, shape):
    result = jnp.zeros(shape, jnp.float32)
    for tap_x in range(3):
        for tap_z in range(3):
            for tap_y in range(3):
                window = padded[
                    :,
                    2 - tap_x : 2 - tap_x + shape[1],
                    2 - tap_z : 2 - tap_z + shape[2],
                    2 - tap_y : 2 - tap_y + shape[3],
                ]
                result = result + jnp.einsum(
                    "oi,oxzy->ixzy",
                    weight[tap_x, tap_z, tap_y],
                    window,
                    preferred_element_type=jnp.float32,
                )
    return result


def taps_from_inputs(grad_field, padded_inputs):
    shape = grad_field.shape
    taps_list = []
    for tap_x in range(3):
        for tap_z in range(3):
            for tap_y in range(3):
                window = padded_inputs[
                    :, tap_x : tap_x + shape[1], tap_z : tap_z + shape[2], tap_y : tap_y + shape[3]
                ]
                taps_list.append(
                    jnp.einsum(
                        "oxzy,ixzy->oi", grad_field, window, preferred_element_type=jnp.float32
                    )
                )
    return jnp.stack(taps_list).reshape(3, 3, 3, shape[0], padded_inputs.shape[0])


def per_device(
    features, pre_first, pre_second, w_first, w_second, w_out, b_out, y_target, k_target
):
    count_sky = lax.axis_size("sky")
    count_los = lax.axis_size("los")
    depth_all = pre_first.shape[2] * count_los
    norm_factor = 1.0 / math.sqrt(features.shape[1] * count_sky * features.shape[3] * depth_all)
    shape = features.shape
    first_wide = pre_first.astype(jnp.float32)
    second_wide = pre_second.astype(jnp.float32)
    hidden_second = jax.nn.silu(second_wide).astype(jnp.bfloat16)
    heads_raw = jnp.einsum(
        "oi,ixzy->oxzy", w_out, hidden_second, preferred_element_type=jnp.float32
    )
    heads_raw = heads_raw + b_out[:, None, None, None]
    pressure = jax.nn.softplus(heads_raw[0])
    density = jax.nn.softplus(heads_raw[1])
    velocity = heads_raw[2]
    y_part = jnp.sum(pressure, axis=1) / depth_all
    k_part = -jnp.sum(density * velocity, axis=1) / depth_all
    y_map, k_map = lax.psum((y_part, k_part), "los")
    y_resid = y_map - y_target
    k_resid = k_map - k_target
    y_resid = y_resid[:, None, :]
    k_resid = k_resid[:, None, :]
    head_grad = jnp.stack(
        (
            y_resid * jax.nn.sigmoid(heads_raw[0]),
            -k_resid * velocity * jax.nn.sigmoid(heads_raw[1]),
            -k_resid * density,
        )
    ).astype(jnp.bfloat16)
    grad_out = (
        jnp.einsum("oxzy,ixzy->oi", head_grad, hidden_second, preferred_element_type=jnp.float32)
        * norm_factor
    )
    grad_bias = jnp.sum(head_grad.astype(jnp.float32), axis=(1, 2, 3)) * norm_factor
    back_second = jnp.einsum("oi,oxzy->ixzy", w_out, head_grad, preferred_element_type=jnp.float32)
    grad_second_pre = (back_second * silu_slope(second_wide)).astype(jnp.bfloat16)
    second_padded = wrap_columns(extended(grad_second_pre, (("sky", 1), ("los", 2)), 1))
    back_first = spread_local(w_second, second_padded, shape)
    grad_first_pre = (back_first * silu_slope(first_wide)).astype(jnp.bfloat16)
    first_padded = wrap_columns(extended(grad_first_pre, (("sky", 1), ("los", 2)), 1))
    grad_features = spread_local(w_first, first_padded, shape).astype(jnp.bfloat16)
    saved_padded = wrap_columns(
        extended(jnp.stack((features, pre_first)), (("sky", 2), ("los", 3)), 1)
    )
    hidden_padded = jax.nn.silu(saved_padded[1].astype(jnp.float32)).astype(jnp.bfloat16)
    grad_second = taps_from_inputs(grad_second_pre, hidden_padded)
    grad_first = taps_from_inputs(grad_first_pre, saved_padded[0])
    grad_first, grad_second, grad_out, grad_bias = lax.psum(
        (grad_first * norm_factor, grad_second * norm_factor, grad_out, grad_bias), ("sky", "los")
    )
    return (grad_features, grad_first, grad_second, grad_out, grad_bias)


def solution(mesh):
    in_specs = (
        P(None, "sky", "los", None),
        P(None, "sky", "los", None),
        P(None, "sky", "los", None),
        P(),
        P(),
        P(),
        P(),
        P("sky", None),
        P("sky", None),
    )
    out_specs = (P(None, "sky", "los", None), P(), P(), P(), P())
    return jax.shard_map(
        per_device, mesh=mesh, in_specs=in_specs, out_specs=out_specs, check_vma=False
    )
```

profile of v0, /device:TPU:0, one launch (start us, length us, event | category | flops | bytes accessed | tf_op | source)
XLA Modules:
  0.0 245.4 jit_solution(12712252060760157756)
XLA Ops:
  7.3 1.0 copy.311
  8.2 0.9 copy.312
  9.2 3.0 %collective-permute-start.8 = (bf16[2,32,1,8,128]{4,1,3,2,0:T(8,128)(2,1)S(1)}, bf16[2,32,1,8,128]{4,1,3,2,0:T(8,128)(2,1)S(1)}, u32[]{:S(2)}, u32[]{:S(2)}) collective-permute-start(bf16[2,32,1,8,128]{4,1,3,2,0:T(8,128)(2,1)S(1)} %get-tuple-element.37), channel_id=1, source_target_pairs={{0,4},{4,8},{8,12},{12,16},{16,20},{20,24},{24,28},{28,0},{1,5},{5... | collective-permute-start | bytes 393224 | tf_op jit(solution)/shard_map/ppermute | solution.py:14
  12.2 3.1 %collective-permute-start.9 = (bf16[2,32,1,8,128]{4,1,3,2,0:T(8,128)(2,1)S(1)}, bf16[2,32,1,8,128]{4,1,3,2,0:T(8,128)(2,1)S(1)}, u32[]{:S(2)}, u32[]{:S(2)}) collective-permute-start(bf16[2,32,1,8,128]{4,1,3,2,0:T(8,128)(2,1)S(1)} %get-tuple-element.38), channel_id=1, source_target_pairs={{4,0},{8,4},{12,8},{16,12},{20,16},{24,20},{28,24},{0,28},{5,1},{9... | collective-permute-start | bytes 393224 | tf_op jit(solution)/shard_map/ppermute | solution.py:17
  15.3 1.0 fusion.100
  16.6 6.3 %all-reduce.2 = (f32[2,128]{1,0:T(2,128)S(1)}, f32[2,128]{1,0:T(2,128)S(1)}) all-reduce(f32[2,128]{1,0:T(2,128)S(1)} %get-tuple-element.54, f32[2,128]{1,0:T(2,128)S(1)} %get-tuple-element.55), channel_id=1, replica_groups=mesh['sky'=8,'los'=4] {'los'}, use_global_device_ids=true, to_apply=%region_3.4 | all-reduce | flops 512 | bytes 4096 | tf_op jit(solution)/shard_map/psum | solution.py:88
  23.4 4.7 %collective-permute-start.1 = (bf16[32,1,8,128]{3,0,2,1:T(8,128)(2,1)S(1)}, bf16[32,1,8,128]{3,0,2,1:T(8,128)(2,1)S(1)}, u32[]{:S(2)}, u32[]{:S(2)}) collective-permute-start(bf16[32,1,8,128]{3,0,2,1:T(8,128)(2,1)S(1)} %get-tuple-element.50), channel_id=1, source_target_pairs={{4,0},{8,4},{12,8},{16,12},{20,16},{24,20},{28,24},{0,28},{5,1},{9... | collective-permute-start | bytes 196616 | tf_op jit(solution)/shard_map/ppermute | solution.py:17
  28.2 2.1 collective-permute-done
  30.4 1.7 collective-permute-start.3
  32.2 39.6 %all-reduce = (f32[3,32]{1,0:T(4,128)}, f32[3]{0:T(128)}) all-reduce(f32[3,32]{1,0:T(4,128)S(1)} %fusion.91, f32[3]{0:T(128)S(1)} %broadcast_multiply_fusion.3), channel_id=1, replica_groups=mesh['sky'=8,'los'=4] {'sky','los'}, use_global_device_ids=true, to_apply=%region_6.7 | all-reduce | flops 99 | bytes 792 | tf_op jit(solution)/shard_map/psum | solution.py:118
  72.0 0.5 pad_maximum_fusion.1
  72.5 0.4 copy-done.2
  75.2 0.2 convolution_add_fusion.25
  78.0 0.2 fusion.32
  79.4 2.6 %collective-permute-start.4 = (bf16[32,1,8,128]{3,0,2,1:T(8,128)(2,1)S(1)}, bf16[32,1,8,128]{3,0,2,1:T(8,128)(2,1)S(1)}, u32[]{:S(2)}, u32[]{:S(2)}) collective-permute-start(bf16[32,1,8,128]{3,0,2,1:T(8,128)(2,1)S(1)} %get-tuple-element.47), channel_id=1, source_target_pairs={{0,4},{4,8},{8,12},{12,16},{16,20},{20,24},{24,28},{28,0},{1,5},{5... | collective-permute-start | bytes 196616 | tf_op jit(solution)/shard_map/ppermute | solution.py:14
  82.0 2.2 collective-permute-start.5
  84.3 1.7 collective-permute-start.11
  86.0 0.5 collective-permute-done.4
  86.6 0.4 collective-permute-done.5
  87.1 1.7 collective-permute-start.7
  88.9 0.3 fusion.349
  89.2 0.8 pad_maximum_fusion
  90.0 0.4 fusion.3
  91.3 0.2 fusion.59
  92.6 0.2 fusion.53
  93.3 0.2 fusion.50
  93.9 0.2 fusion.47
  94.6 0.2 fusion.44
  95.2 0.3 fusion.41
  95.9 0.2 fusion.38
  96.4 0.8 broadcast_multiply_fusion
  98.0 0.2 fusion.86
  98.7 0.2 fusion.83
  99.4 0.2 fusion.80
  100.0 0.2 fusion.77
  100.7 0.3 fusion.74
  101.3 0.2 fusion.71
  102.0 0.2 fusion.68
  102.7 0.2 fusion.65
  103.2 0.8 broadcast_multiply_fusion.1
  104.3 0.5 pad_maximum_fusion.2
  104.8 0.4 copy-done.1
  107.5 0.2 convolution_add_fusion.12
  110.3 0.2 fusion.30
  111.4 0.7 copy.134
  112.1 122.8 %all-reduce.5.cloned.1.call-done = (f32[3,3,3,32,32]{4,3,2,1,0:T(8,128)}, f32[3,3,3,32,32]{4,3,2,1,0:T(8,128)}) async-done(((f32[3,3,3,32,32]{4,3,2,1,0:T(8,128)}, f32[3,3,3,32,32]{4,3,2,1,0:T(8,128)}), (f32[3,3,3,32,32]{4,3,2,1,0:T(8,128)}, f32[3,3,3,32,32]{4,3,2,1,0:T(8,128)})) %all-reduce.5.cloned.1.call-update) | async-done | bytes 221200 | tf_op jit(solution)/shard_map/psum | solution.py:118
  235.0 1.8 copy.367
  236.8 1.8 copy.368
  (143 shorter events, 21.2 us)
Async XLA Ops:
  7.2 9.2 %copy-start = (bf16[3,32]{1,0:T(4,128)(2,1)S(1)}, bf16[3,32]{1,0:T(4,128)(2,1)}, u32[]{:S(2)}) copy-start(bf16[3,32]{1,0:T(4,128)(2,1)} %param.14) | copy-start | bytes 580
  7.2 15.9 %copy-start.3 = (bf16[32,2,8,128]{3,2,1,0:T(8,128)(2,1)S(1)}, bf16[32,2,8,128]{3,2,1,0:T(8,128)(2,1)}, u32[]{:S(2)}) copy-start(bf16[32,2,8,128]{3,2,1,0:T(8,128)(2,1)} %param.11) | copy-start | bytes 393220
  7.2 9.3 %copy-start.7 = (f32[3]{0:T(128)S(1)}, f32[3]{0:T(128)}, u32[]{:S(2)}) copy-start(f32[3]{0:T(128)} %param.15) | copy-start | bytes 40
  7.2 15.7 %copy-start.5 = (f32[2,128]{1,0:T(2,128)S(1)}, f32[2,128]{1,0:T(2,128)}, u32[]{:S(2)}) copy-start(f32[2,128]{1,0:T(2,128)} %param.16) | copy-start | bytes 3076
  7.2 15.7 %copy-start.6 = (f32[2,128]{1,0:T(2,128)S(1)}, f32[2,128]{1,0:T(2,128)}, u32[]{:S(2)}) copy-start(f32[2,128]{1,0:T(2,128)} %param.17) | copy-start | bytes 3076
  7.2 227.8 %all-reduce.5.cloned.1.call-start = ((), (), s32[]{:S(2)}) async-start(), calls=%async_computation | async-start | bytes 1769472 | tf_op jit(solution)/shard_map/psum | solution.py:118
  9.2 75.0 %collective-permute-start.8 = (bf16[2,32,1,8,128]{4,1,3,2,0:T(8,128)(2,1)S(1)}, bf16[2,32,1,8,128]{4,1,3,2,0:T(8,128)(2,1)S(1)}, u32[]{:S(2)}, u32[]{:S(2)}) collective-permute-start(bf16[2,32,1,8,128]{4,1,3,2,0:T(8,128)(2,1)S(1)} %get-tuple-element.37), channel_id=1, source_target_pairs={{0,4},{4,8},{8,12},{12,16},{16,20},{20,24},{24,28},{28,0},{1,5},{5... | collective-permute-start | bytes 393224 | tf_op jit(solution)/shard_map/ppermute | solution.py:14
  12.2 72.0 %collective-permute-start.9 = (bf16[2,32,1,8,128]{4,1,3,2,0:T(8,128)(2,1)S(1)}, bf16[2,32,1,8,128]{4,1,3,2,0:T(8,128)(2,1)S(1)}, u32[]{:S(2)}, u32[]{:S(2)}) collective-permute-start(bf16[2,32,1,8,128]{4,1,3,2,0:T(8,128)(2,1)S(1)} %get-tuple-element.38), channel_id=1, source_target_pairs={{4,0},{8,4},{12,8},{16,12},{20,16},{24,20},{28,24},{0,28},{5,1},{9... | collective-permute-start | bytes 393224 | tf_op jit(solution)/shard_map/ppermute | solution.py:17
  23.3 7.0 %collective-permute-start = (bf16[32,1,8,128]{3,0,2,1:T(8,128)(2,1)S(1)}, bf16[32,1,8,128]{3,0,2,1:T(8,128)(2,1)S(1)}, u32[]{:S(2)}, u32[]{:S(2)}) collective-permute-start(bf16[32,1,8,128]{3,0,2,1:T(8,128)(2,1)S(1)} %get-tuple-element.49), channel_id=1, source_target_pairs={{0,4},{4,8},{8,12},{12,16},{16,20},{20,24},{24,28},{28,0},{1,5},{5... | collective-permute-start | bytes 196616 | tf_op jit(solution)/shard_map/ppermute | solution.py:14
  23.4 7.0 %collective-permute-start.1 = (bf16[32,1,8,128]{3,0,2,1:T(8,128)(2,1)S(1)}, bf16[32,1,8,128]{3,0,2,1:T(8,128)(2,1)S(1)}, u32[]{:S(2)}, u32[]{:S(2)}) collective-permute-start(bf16[32,1,8,128]{3,0,2,1:T(8,128)(2,1)S(1)} %get-tuple-element.50), channel_id=1, source_target_pairs={{4,0},{8,4},{12,8},{16,12},{20,16},{24,20},{28,24},{0,28},{5,1},{9... | collective-permute-start | bytes 196616 | tf_op jit(solution)/shard_map/ppermute | solution.py:17
  30.4 41.4 %collective-permute-start.2 = (bf16[32,4,1,128]{3,0,2,1:T(8,128)(2,1)S(1)}, bf16[32,4,1,128]{3,0,2,1:T(8,128)(2,1)S(1)}, u32[]{:S(2)}, u32[]{:S(2)}) collective-permute-start(bf16[32,4,1,128]{3,0,2,1:T(8,128)(2,1)S(1)} %get-tuple-element.45), channel_id=1, source_target_pairs={{0,1},{1,2},{2,3},{3,0},{4,5},{5,6},{6,7},{7,4},{8,9},{9,10},{10,1... | collective-permute-start | bytes 98312 | tf_op jit(solution)/shard_map/ppermute | solution.py:14
  30.4 41.4 %collective-permute-start.3 = (bf16[32,4,1,128]{3,0,2,1:T(8,128)(2,1)S(1)}, bf16[32,4,1,128]{3,0,2,1:T(8,128)(2,1)S(1)}, u32[]{:S(2)}, u32[]{:S(2)}) collective-permute-start(bf16[32,4,1,128]{3,0,2,1:T(8,128)(2,1)S(1)} %get-tuple-element.46), channel_id=1, source_target_pairs={{1,0},{2,1},{3,2},{0,3},{5,4},{6,5},{7,6},{4,7},{9,8},{10,9},{11,1... | collective-permute-start | bytes 98312 | tf_op jit(solution)/shard_map/ppermute | solution.py:17
  72.0 0.9 copy-start.2
  78.3 0.9 copy-start.4
  79.4 7.1 %collective-permute-start.4 = (bf16[32,1,8,128]{3,0,2,1:T(8,128)(2,1)S(1)}, bf16[32,1,8,128]{3,0,2,1:T(8,128)(2,1)S(1)}, u32[]{:S(2)}, u32[]{:S(2)}) collective-permute-start(bf16[32,1,8,128]{3,0,2,1:T(8,128)(2,1)S(1)} %get-tuple-element.47), channel_id=1, source_target_pairs={{0,4},{4,8},{8,12},{12,16},{16,20},{20,24},{24,28},{28,0},{1,5},{5... | collective-permute-start | bytes 196616 | tf_op jit(solution)/shard_map/ppermute | solution.py:14
  82.0 5.0 %collective-permute-start.5 = (bf16[32,1,8,128]{3,0,2,1:T(8,128)(2,1)S(1)}, bf16[32,1,8,128]{3,0,2,1:T(8,128)(2,1)S(1)}, u32[]{:S(2)}, u32[]{:S(2)}) collective-permute-start(bf16[32,1,8,128]{3,0,2,1:T(8,128)(2,1)S(1)} %get-tuple-element.48), channel_id=1, source_target_pairs={{4,0},{8,4},{12,8},{16,12},{20,16},{24,20},{28,24},{0,28},{5,1},{9... | collective-permute-start | bytes 196616 | tf_op jit(solution)/shard_map/ppermute | solution.py:17
  84.2 4.6 %collective-permute-start.10 = (bf16[2,32,4,1,128]{4,1,3,2,0:T(8,128)(2,1)S(1)}, bf16[2,32,4,1,128]{4,1,3,2,0:T(8,128)(2,1)S(1)}, u32[]{:S(2)}, u32[]{:S(2)}) collective-permute-start(bf16[2,32,4,1,128]{4,1,3,2,0:T(8,128)(2,1)S(1)} %get-tuple-element.27), channel_id=1, source_target_pairs={{0,1},{1,2},{2,3},{3,0},{4,5},{5,6},{6,7},{7,4},{8,9},{9,10},{10,1... | collective-permute-start | bytes 196616 | tf_op jit(solution)/shard_map/ppermute | solution.py:14
  84.3 4.5 %collective-permute-start.11 = (bf16[2,32,4,1,128]{4,1,3,2,0:T(8,128)(2,1)S(1)}, bf16[2,32,4,1,128]{4,1,3,2,0:T(8,128)(2,1)S(1)}, u32[]{:S(2)}, u32[]{:S(2)}) collective-permute-start(bf16[2,32,4,1,128]{4,1,3,2,0:T(8,128)(2,1)S(1)} %get-tuple-element.28), channel_id=1, source_target_pairs={{1,0},{2,1},{3,2},{0,3},{5,4},{6,5},{7,6},{4,7},{9,8},{10,9},{11,1... | collective-permute-start | bytes 196616 | tf_op jit(solution)/shard_map/ppermute | solution.py:17
  87.0 17.0 %collective-permute-start.6 = (bf16[32,4,1,128]{3,0,2,1:T(8,128)(2,1)S(1)}, bf16[32,4,1,128]{3,0,2,1:T(8,128)(2,1)S(1)}, u32[]{:S(2)}, u32[]{:S(2)}) collective-permute-start(bf16[32,4,1,128]{3,0,2,1:T(8,128)(2,1)S(1)} %get-tuple-element.41), channel_id=1, source_target_pairs={{0,1},{1,2},{2,3},{3,0},{4,5},{5,6},{6,7},{7,4},{8,9},{9,10},{10,1... | collective-permute-start | bytes 98312 | tf_op jit(solution)/shard_map/ppermute | solution.py:14
  87.1 16.9 %collective-permute-start.7 = (bf16[32,4,1,128]{3,0,2,1:T(8,128)(2,1)S(1)}, bf16[32,4,1,128]{3,0,2,1:T(8,128)(2,1)S(1)}, u32[]{:S(2)}, u32[]{:S(2)}) collective-permute-start(bf16[32,4,1,128]{3,0,2,1:T(8,128)(2,1)S(1)} %get-tuple-element.42), channel_id=1, source_target_pairs={{1,0},{2,1},{3,2},{0,3},{5,4},{6,5},{7,6},{4,7},{9,8},{10,9},{11,1... | collective-permute-start | bytes 98312 | tf_op jit(solution)/shard_map/ppermute | solution.py:17
  104.3 0.9 copy-start.1
Sparse Core Ops, SparseCore 0:
  104.1 130.8 all-reduce.4
where the time goes:
time: 246 us; the launch traced here: 245 us
  waiting for transfers between devices  126 us (51%)
  blocking collectives  45.9 us (19%)
  matrix products  24.4 us (10%)
  starting transfers between devices  21.1 us (9%)
  between operations  14.7 us (6%)
  local copies, waits for them, and re-layouts  8.01 us (3%)
  other arithmetic  5.42 us (2%)
    psum x1, waiting for transfers between devices, per_device(): lax.psum((grad_first * norm_factor, grad_second * norm_factor, grad_out,...  123 us
    psum x1, blocking collectives, per_device(): lax.psum((grad_first * norm_factor, grad_second * norm_factor, grad_out,...  39.6 us
    ppermute x6, starting transfers between devices, extended(): lax.ppermute(lax.slice_in_dim(block, 0, width, axis=dim), axis, backward)  15.2 us
    dot_general x54, matrix products, spread_local(): jnp.einsum('oi,oxzy->ixzy', weight[tap_x, tap_z, tap_y], window, preferre...  12 us
    dot_general x54, matrix products, taps_from_inputs(): jnp.einsum('oxzy,ixzy->oi', grad_field, window, preferred_element_type=jn...  11.9 us
    unnamed x21, local copies, waits for them, and re-layouts  7.35 us
    psum x1, blocking collectives, per_device(): y_map, k_map = lax.psum((y_part, k_part), 'los')  6.31 us
    ppermute x6, starting transfers between devices, extended(): lax.ppermute(lax.slice_in_dim(block, block.shape[dim] - width, None, axis...  5.83 us
  transfers between devices with their start and end apart: 13, of which 4 were waited for; matrix products, arithmetic and copies ran while one was open for 13% of the time, Pallas kernels for 0%

commit v1 on v0

--- a/solution.py
+++ b/solution.py
@@ -116,7 +116,8 @@
     grad_second = taps_from_inputs(grad_second_pre, hidden_padded)
     grad_first = taps_from_inputs(grad_first_pre, saved_padded[0])
     grad_first, grad_second, grad_out, grad_bias = lax.psum(
-        (grad_first * norm_factor, grad_second * norm_factor, grad_out, grad_bias), ("sky", "los")
+        lax.psum((grad_first * norm_factor, grad_second * norm_factor, grad_out, grad_bias), "los"),
+        "sky",
     )
     return (grad_features, grad_first, grad_second, grad_out, grad_bias)
 

time: 246 us -> 219 us (0.89)
  waiting for transfers between devices: 126 us -> 110 us
  blocking collectives: 45.9 us -> 34.3 us
    psum x1, waiting for transfers between devices: 123 us -> 29 us  [per_device(): lax.psum((grad_first * norm_factor, grad_second * norm_factor, grad_out,...]
    psum x0 -> x1, waiting for transfers between devices: none -> 78.9 us  [per_device(): lax.psum(lax.psum((grad_first * norm_factor, grad_second * norm_factor, g...]
    psum x1, blocking collectives: 39.6 us -> 5.64 us  [per_device(): lax.psum((grad_first * norm_factor, grad_second * norm_factor, grad_out,...]
    psum x0 -> x1, blocking collectives: none -> 22.4 us  [per_device(): lax.psum(lax.psum((grad_first * norm_factor, grad_second * norm_factor, g...]
    ppermute x6, starting transfers between devices: 5.83 us -> 3.31 us  [extended(): lax.ppermute(lax.slice_in_dim(block, block.shape[dim] - width, None, axis...]
    ppermute x6, starting transfers between devices: 15.2 us -> 17.7 us  [extended(): lax.ppermute(lax.slice_in_dim(block, 0, width, axis=dim), axis, backward)]
  transfers between devices with their start and end apart: 13 -> 14, of which waited for: 4 -> 4; matrix products, arithmetic and copies ran while one was open for 13% -> 14% of each run, Pallas kernels for 0% -> 0%
where the time goes in v1:
time: 219 us
  waiting for transfers between devices  110 us (50%)
  blocking collectives  34.3 us (16%)
  matrix products  24.4 us (11%)
  starting transfers between devices  21.3 us (10%)
  between operations  14.7 us (7%)
  local copies, waits for them, and re-layouts  8 us (4%)
  other arithmetic  5.42 us (2%)
    psum x1, waiting for transfers between devices, per_device(): lax.psum(lax.psum((grad_first * norm_factor, grad_second * norm_factor, g...  78.9 us
    psum x1, waiting for transfers between devices, per_device(): lax.psum((grad_first * norm_factor, grad_second * norm_factor, grad_out,...  29 us
    psum x1, blocking collectives, per_device(): lax.psum(lax.psum((grad_first * norm_factor, grad_second * norm_factor, g...  22.4 us
    ppermute x6, starting transfers between devices, extended(): lax.ppermute(lax.slice_in_dim(block, 0, width, axis=dim), axis, backward)  17.7 us
    dot_general x54, matrix products, spread_local(): jnp.einsum('oi,oxzy->ixzy', weight[tap_x, tap_z, tap_y], window, preferre...  12 us
    dot_general x54, matrix products, taps_from_inputs(): jnp.einsum('oxzy,ixzy->oi', grad_field, window, preferred_element_type=jn...  11.9 us
    unnamed x21, local copies, waits for them, and re-layouts  7.35 us
    psum x1, blocking collectives, per_device(): y_map, k_map = lax.psum((y_part, k_part), 'los')  6.31 us
  transfers between devices with their start and end apart: 14, of which 4 were waited for; matrix products, arithmetic and copies ran while one was open for 14% of the time, Pallas kernels for 0%

profile of v1, /device:TPU:0, one launch (start us, length us, event | category | flops | bytes accessed | tf_op | source)
XLA Modules:
  0.0 218.5 jit_solution(4682568609867258302)
XLA Ops:
  7.3 1.0 copy.311
  8.2 0.9 copy.312
  9.2 3.0 %collective-permute-start.8 = (bf16[2,32,1,8,128]{4,1,3,2,0:T(8,128)(2,1)S(1)}, bf16[2,32,1,8,128]{4,1,3,2,0:T(8,128)(2,1)S(1)}, u32[]{:S(2)}, u32[]{:S(2)}) collective-permute-start(bf16[2,32,1,8,128]{4,1,3,2,0:T(8,128)(2,1)S(1)} %get-tuple-element.41), channel_id=1, source_target_pairs={{0,4},{4,8},{8,12},{12,16},{16,20},{20,24},{24,28},{28,0},{1,5},{5... | collective-permute-start | bytes 393224 | tf_op jit(solution)/shard_map/ppermute | solution.py:14
  12.2 3.1 %collective-permute-start.9 = (bf16[2,32,1,8,128]{4,1,3,2,0:T(8,128)(2,1)S(1)}, bf16[2,32,1,8,128]{4,1,3,2,0:T(8,128)(2,1)S(1)}, u32[]{:S(2)}, u32[]{:S(2)}) collective-permute-start(bf16[2,32,1,8,128]{4,1,3,2,0:T(8,128)(2,1)S(1)} %get-tuple-element.42), channel_id=1, source_target_pairs={{4,0},{8,4},{12,8},{16,12},{20,16},{24,20},{28,24},{0,28},{5,1},{9... | collective-permute-start | bytes 393224 | tf_op jit(solution)/shard_map/ppermute | solution.py:17
  15.3 1.0 fusion.100
  16.6 6.3 %all-reduce.3 = (f32[2,128]{1,0:T(2,128)S(1)}, f32[2,128]{1,0:T(2,128)S(1)}) all-reduce(f32[2,128]{1,0:T(2,128)S(1)} %get-tuple-element.58, f32[2,128]{1,0:T(2,128)S(1)} %get-tuple-element.59), channel_id=1, replica_groups=mesh['sky'=8,'los'=4] {'los'}, use_global_device_ids=true, to_apply=%region_3.4 | all-reduce | flops 512 | bytes 4096 | tf_op jit(solution)/shard_map/psum | solution.py:88
  23.4 4.7 %collective-permute-start.1 = (bf16[32,1,8,128]{3,0,2,1:T(8,128)(2,1)S(1)}, bf16[32,1,8,128]{3,0,2,1:T(8,128)(2,1)S(1)}, u32[]{:S(2)}, u32[]{:S(2)}) collective-permute-start(bf16[32,1,8,128]{3,0,2,1:T(8,128)(2,1)S(1)} %get-tuple-element.54), channel_id=1, source_target_pairs={{4,0},{8,4},{12,8},{16,12},{20,16},{24,20},{28,24},{0,28},{5,1},{9... | collective-permute-start | bytes 196616 | tf_op jit(solution)/shard_map/ppermute | solution.py:17
  28.2 2.1 collective-permute-done
  30.4 1.7 collective-permute-start.3
  32.2 5.6 %all-reduce.2 = (f32[3,32]{1,0:T(4,128)S(1)}, f32[3]{0:T(128)S(1)}) all-reduce(f32[3,32]{1,0:T(4,128)S(1)} %fusion.91, f32[3]{0:T(128)S(1)} %broadcast_multiply_fusion.3), channel_id=1, replica_groups=mesh['sky'=8,'los'=4] {'los'}, use_global_device_ids=true, to_apply=%region_8.9 | all-reduce | flops 99 | bytes 792 | tf_op jit(solution)/shard_map/psum | solution.py:119
  37.8 22.4 %all-reduce = (f32[3,32]{1,0:T(4,128)}, f32[3]{0:T(128)}) all-reduce(f32[3,32]{1,0:T(4,128)S(1)} %get-tuple-element.21, f32[3]{0:T(128)S(1)} %get-tuple-element.22), channel_id=1, replica_groups=mesh['sky'=8,'los'=4] {'sky'}, use_global_device_ids=true, to_apply=%region_9.10 | all-reduce | flops 99 | bytes 792 | tf_op jit(solution)/shard_map/psum | solution.py:118
  60.4 0.5 pad_maximum_fusion.1
  60.9 0.4 copy-done.2
  63.6 0.2 convolution_add_fusion.25
  66.4 0.2 fusion.32
  67.9 4.7 %collective-permute-start.5 = (bf16[32,1,8,128]{3,0,2,1:T(8,128)(2,1)S(1)}, bf16[32,1,8,128]{3,0,2,1:T(8,128)(2,1)S(1)}, u32[]{:S(2)}, u32[]{:S(2)}) collective-permute-start(bf16[32,1,8,128]{3,0,2,1:T(8,128)(2,1)S(1)} %get-tuple-element.52), channel_id=1, source_target_pairs={{4,0},{8,4},{12,8},{16,12},{20,16},{24,20},{28,24},{0,28},{5,1},{9... | collective-permute-start | bytes 196616 | tf_op jit(solution)/shard_map/ppermute | solution.py:17
  72.7 1.7 collective-permute-start.11
  74.4 0.4 collective-permute-done.4
  74.9 1.7 collective-permute-start.7
  76.8 0.3 fusion.349
  77.1 0.8 pad_maximum_fusion
  77.9 0.4 fusion.3
  79.1 0.2 fusion.59
  79.8 0.3 fusion.56
  80.5 0.2 fusion.53
  81.1 0.2 fusion.50
  81.8 0.2 fusion.47
  82.5 0.2 fusion.44
  83.8 0.2 fusion.38
  84.3 0.8 broadcast_multiply_fusion
  85.9 0.3 fusion.86
  86.6 0.2 fusion.83
  87.2 0.2 fusion.80
  87.5 0.3 fusion.79
  87.9 0.3 fusion.77
  89.2 0.3 fusion.71
  90.1 0.3 fusion.67
  90.6 0.2 fusion.65
  91.0 0.8 broadcast_multiply_fusion.1
  92.4 0.5 pad_maximum_fusion.2
  92.9 0.4 copy-done.1
  95.6 0.2 convolution_add_fusion.12
  98.4 0.2 fusion.30
  99.3 29.0 %all-reduce.10.cloned.1.call-done = (f32[3,3,3,32,32]{4,3,2,1,0:T(8,128)}, f32[3,3,3,32,32]{4,3,2,1,0:T(8,128)}) async-done(((f32[3,3,3,32,32]{4,3,2,1,0:T(8,128)}, f32[3,3,3,32,32]{4,3,2,1,0:T(8,128)}), (f32[3,3,3,32,32]{4,3,2,1,0:T(8,128)}, f32[3,3,3,32,32]{4,3,2,1,0:T(8,128)})) %all-reduce.10.cloned.1.call-update) | async-done | bytes 221200 | tf_op jit(solution)/shard_map/psum | solution.py:119
  128.5 0.7 copy.134
  129.2 78.9 %all-reduce.8.cloned.1.call-done = (f32[3,3,3,32,32]{4,3,2,1,0:T(8,128)}, f32[3,3,3,32,32]{4,3,2,1,0:T(8,128)}) async-done(((f32[3,3,3,32,32]{4,3,2,1,0:T(8,128)}, f32[3,3,3,32,32]{4,3,2,1,0:T(8,128)}), (f32[3,3,3,32,32]{4,3,2,1,0:T(8,128)}, f32[3,3,3,32,32]{4,3,2,1,0:T(8,128)})) %all-reduce.8.cloned.1.call-update) | async-done | bytes 221200 | tf_op jit(solution)/shard_map/psum | solution.py:118
  208.1 1.8 copy.369
  209.9 1.8 copy.370
  (147 shorter events, 21.5 us)
Async XLA Ops:
  7.2 9.2 %copy-start = (bf16[3,32]{1,0:T(4,128)(2,1)S(1)}, bf16[3,32]{1,0:T(4,128)(2,1)}, u32[]{:S(2)}) copy-start(bf16[3,32]{1,0:T(4,128)(2,1)} %param.14) | copy-start | bytes 580
  7.2 15.9 %copy-start.3 = (bf16[32,2,8,128]{3,2,1,0:T(8,128)(2,1)S(1)}, bf16[32,2,8,128]{3,2,1,0:T(8,128)(2,1)}, u32[]{:S(2)}) copy-start(bf16[32,2,8,128]{3,2,1,0:T(8,128)(2,1)} %param.11) | copy-start | bytes 393220
  7.2 9.3 %copy-start.7 = (f32[3]{0:T(128)S(1)}, f32[3]{0:T(128)}, u32[]{:S(2)}) copy-start(f32[3]{0:T(128)} %param.15) | copy-start | bytes 40
  7.2 15.7 %copy-start.5 = (f32[2,128]{1,0:T(2,128)S(1)}, f32[2,128]{1,0:T(2,128)}, u32[]{:S(2)}) copy-start(f32[2,128]{1,0:T(2,128)} %param.16) | copy-start | bytes 3076
  7.2 15.7 %copy-start.6 = (f32[2,128]{1,0:T(2,128)S(1)}, f32[2,128]{1,0:T(2,128)}, u32[]{:S(2)}) copy-start(f32[2,128]{1,0:T(2,128)} %param.17) | copy-start | bytes 3076
  7.2 121.1 %all-reduce.10.cloned.1.call-start = ((), (), s32[]{:S(2)}) async-start(), calls=%async_computation.1 | async-start | bytes 1769472 | tf_op jit(solution)/shard_map/psum | solution.py:119
  9.2 63.4 %collective-permute-start.8 = (bf16[2,32,1,8,128]{4,1,3,2,0:T(8,128)(2,1)S(1)}, bf16[2,32,1,8,128]{4,1,3,2,0:T(8,128)(2,1)S(1)}, u32[]{:S(2)}, u32[]{:S(2)}) collective-permute-start(bf16[2,32,1,8,128]{4,1,3,2,0:T(8,128)(2,1)S(1)} %get-tuple-element.41), channel_id=1, source_target_pairs={{0,4},{4,8},{8,12},{12,16},{16,20},{20,24},{24,28},{28,0},{1,5},{5... | collective-permute-start | bytes 393224 | tf_op jit(solution)/shard_map/ppermute | solution.py:14
  12.2 60.4 %collective-permute-start.9 = (bf16[2,32,1,8,128]{4,1,3,2,0:T(8,128)(2,1)S(1)}, bf16[2,32,1,8,128]{4,1,3,2,0:T(8,128)(2,1)S(1)}, u32[]{:S(2)}, u32[]{:S(2)}) collective-permute-start(bf16[2,32,1,8,128]{4,1,3,2,0:T(8,128)(2,1)S(1)} %get-tuple-element.42), channel_id=1, source_target_pairs={{4,0},{8,4},{12,8},{16,12},{20,16},{24,20},{28,24},{0,28},{5,1},{9... | collective-permute-start | bytes 393224 | tf_op jit(solution)/shard_map/ppermute | solution.py:17
  23.3 7.0 %collective-permute-start = (bf16[32,1,8,128]{3,0,2,1:T(8,128)(2,1)S(1)}, bf16[32,1,8,128]{3,0,2,1:T(8,128)(2,1)S(1)}, u32[]{:S(2)}, u32[]{:S(2)}) collective-permute-start(bf16[32,1,8,128]{3,0,2,1:T(8,128)(2,1)S(1)} %get-tuple-element.53), channel_id=1, source_target_pairs={{0,4},{4,8},{8,12},{12,16},{16,20},{20,24},{24,28},{28,0},{1,5},{5... | collective-permute-start | bytes 196616 | tf_op jit(solution)/shard_map/ppermute | solution.py:14
  23.4 7.0 %collective-permute-start.1 = (bf16[32,1,8,128]{3,0,2,1:T(8,128)(2,1)S(1)}, bf16[32,1,8,128]{3,0,2,1:T(8,128)(2,1)S(1)}, u32[]{:S(2)}, u32[]{:S(2)}) collective-permute-start(bf16[32,1,8,128]{3,0,2,1:T(8,128)(2,1)S(1)} %get-tuple-element.54), channel_id=1, source_target_pairs={{4,0},{8,4},{12,8},{16,12},{20,16},{24,20},{28,24},{0,28},{5,1},{9... | collective-permute-start | bytes 196616 | tf_op jit(solution)/shard_map/ppermute | solution.py:17
  30.4 29.8 %collective-permute-start.2 = (bf16[32,4,1,128]{3,0,2,1:T(8,128)(2,1)S(1)}, bf16[32,4,1,128]{3,0,2,1:T(8,128)(2,1)S(1)}, u32[]{:S(2)}, u32[]{:S(2)}) collective-permute-start(bf16[32,4,1,128]{3,0,2,1:T(8,128)(2,1)S(1)} %get-tuple-element.49), channel_id=1, source_target_pairs={{0,1},{1,2},{2,3},{3,0},{4,5},{5,6},{6,7},{7,4},{8,9},{9,10},{10,1... | collective-permute-start | bytes 98312 | tf_op jit(solution)/shard_map/ppermute | solution.py:14
  30.4 29.8 %collective-permute-start.3 = (bf16[32,4,1,128]{3,0,2,1:T(8,128)(2,1)S(1)}, bf16[32,4,1,128]{3,0,2,1:T(8,128)(2,1)S(1)}, u32[]{:S(2)}, u32[]{:S(2)}) collective-permute-start(bf16[32,4,1,128]{3,0,2,1:T(8,128)(2,1)S(1)} %get-tuple-element.50), channel_id=1, source_target_pairs={{1,0},{2,1},{3,2},{0,3},{5,4},{6,5},{7,6},{4,7},{9,8},{10,9},{11,1... | collective-permute-start | bytes 98312 | tf_op jit(solution)/shard_map/ppermute | solution.py:17
  60.4 0.9 copy-start.2
  66.7 0.9 copy-start.4
  67.8 7.0 %collective-permute-start.4 = (bf16[32,1,8,128]{3,0,2,1:T(8,128)(2,1)S(1)}, bf16[32,1,8,128]{3,0,2,1:T(8,128)(2,1)S(1)}, u32[]{:S(2)}, u32[]{:S(2)}) collective-permute-start(bf16[32,1,8,128]{3,0,2,1:T(8,128)(2,1)S(1)} %get-tuple-element.51), channel_id=1, source_target_pairs={{0,4},{4,8},{8,12},{12,16},{16,20},{20,24},{24,28},{28,0},{1,5},{5... | collective-permute-start | bytes 196616 | tf_op jit(solution)/shard_map/ppermute | solution.py:14
  67.9 7.0 %collective-permute-start.5 = (bf16[32,1,8,128]{3,0,2,1:T(8,128)(2,1)S(1)}, bf16[32,1,8,128]{3,0,2,1:T(8,128)(2,1)S(1)}, u32[]{:S(2)}, u32[]{:S(2)}) collective-permute-start(bf16[32,1,8,128]{3,0,2,1:T(8,128)(2,1)S(1)} %get-tuple-element.52), channel_id=1, source_target_pairs={{4,0},{8,4},{12,8},{16,12},{20,16},{24,20},{28,24},{0,28},{5,1},{9... | collective-permute-start | bytes 196616 | tf_op jit(solution)/shard_map/ppermute | solution.py:17
  72.6 4.0 %collective-permute-start.10 = (bf16[2,32,4,1,128]{4,1,3,2,0:T(8,128)(2,1)S(1)}, bf16[2,32,4,1,128]{4,1,3,2,0:T(8,128)(2,1)S(1)}, u32[]{:S(2)}, u32[]{:S(2)}) collective-permute-start(bf16[2,32,4,1,128]{4,1,3,2,0:T(8,128)(2,1)S(1)} %get-tuple-element.31), channel_id=1, source_target_pairs={{0,1},{1,2},{2,3},{3,0},{4,5},{5,6},{6,7},{7,4},{8,9},{9,10},{10,1... | collective-permute-start | bytes 196616 | tf_op jit(solution)/shard_map/ppermute | solution.py:14
  72.7 4.0 %collective-permute-start.11 = (bf16[2,32,4,1,128]{4,1,3,2,0:T(8,128)(2,1)S(1)}, bf16[2,32,4,1,128]{4,1,3,2,0:T(8,128)(2,1)S(1)}, u32[]{:S(2)}, u32[]{:S(2)}) collective-permute-start(bf16[2,32,4,1,128]{4,1,3,2,0:T(8,128)(2,1)S(1)} %get-tuple-element.32), channel_id=1, source_target_pairs={{1,0},{2,1},{3,2},{0,3},{5,4},{6,5},{7,6},{4,7},{9,8},{10,9},{11,1... | collective-permute-start | bytes 196616 | tf_op jit(solution)/shard_map/ppermute | solution.py:17
  74.9 17.2 %collective-permute-start.6 = (bf16[32,4,1,128]{3,0,2,1:T(8,128)(2,1)S(1)}, bf16[32,4,1,128]{3,0,2,1:T(8,128)(2,1)S(1)}, u32[]{:S(2)}, u32[]{:S(2)}) collective-permute-start(bf16[32,4,1,128]{3,0,2,1:T(8,128)(2,1)S(1)} %get-tuple-element.45), channel_id=1, source_target_pairs={{0,1},{1,2},{2,3},{3,0},{4,5},{5,6},{6,7},{7,4},{8,9},{9,10},{10,1... | collective-permute-start | bytes 98312 | tf_op jit(solution)/shard_map/ppermute | solution.py:14
  74.9 17.2 %collective-permute-start.7 = (bf16[32,4,1,128]{3,0,2,1:T(8,128)(2,1)S(1)}, bf16[32,4,1,128]{3,0,2,1:T(8,128)(2,1)S(1)}, u32[]{:S(2)}, u32[]{:S(2)}) collective-permute-start(bf16[32,4,1,128]{3,0,2,1:T(8,128)(2,1)S(1)} %get-tuple-element.46), channel_id=1, source_target_pairs={{1,0},{2,1},{3,2},{0,3},{5,4},{6,5},{7,6},{4,7},{9,8},{10,9},{11,1... | collective-permute-start | bytes 98312 | tf_op jit(solution)/shard_map/ppermute | solution.py:17
  91.9 116.2 %all-reduce.8.cloned.1.call-start = ((), (), s32[]{:S(2)}) async-start(), calls=%async_computation | async-start | bytes 1769472 | tf_op jit(solution)/shard_map/psum | solution.py:118
  92.4 0.9 copy-start.1
Sparse Core Ops, SparseCore 0:
  92.0 36.2 all-reduce.9
  131.7 76.2 all-reduce.7
